TPU v7x, 256 devices: a whole 4x4x8 slice. The times are simulated.
256 devices in a mesh: band: 8 (over x_hi, y), dom: 32 (over x_lo, z, core).
Axes of the slice: x: 4 (x_hi: 2, x_lo: 2; x = x_hi * 2 + x_lo), y: 4, z: 8, core: 2. Of those that a mesh axis runs over, the one named last changes fastest.
Arguments:
- wave: bfloat16 [192, 19, 13, 2048], P('dom', None, None, 'band'), parts along dimension 3, may hold values from -6 to 6
- kinetic: bfloat16 [343, 343], replicated, may hold values from -1 to 1, as said below
- cell_scale: float32 [192], P('dom'), may hold values from 0.5 to 2
- potential: float32 [192, 19, 13], P('dom'), may hold values from 0.2 to 2
- proj_values: bfloat16 [512, 343], P('dom'), may hold values from -0.23925781 to 0.23925781
- piece_cell: int32 [512], P('dom'), may hold values from 0 to 5
- piece_proj: int32 [512], P('dom'), may hold values from 0 to 255
- coupling: float32 [256], replicated, may hold values from 0.5 to 2
- center: float32 [1], replicated, may hold values from 9 to 11
- halfwidth: float32 [1], replicated, may hold values from 14 to 18
Outputs:
- filtered: float32 [192, 19, 13, 2048], P('dom', None, None, 'band'), parts along dimension 3
There are 8 independent parts, one for each index of `band`. A program takes and returns all parts, laid end to end along the dimension named above; an argument that names none is the same for every part. Nothing has to cross between parts.
Inputs may be any that keep to these rules, and one draw needn't show every extreme that they name: kinetic is symmetric.
All inputs are finite; a program needn't handle non-finite values.
Results may differ from a plain program's by a relative error of at most 0.0014.
Values may be sent and summed in bfloat16 or wider, within the bound.
No kernel may reach another device: no remote copies, remote signals or barrier semaphores. Data moves between devices by JAX's collectives and lax.ppermute only.
A program may use at most 64 MiB of HBM per device.

v0:
```python
import jax
import jax.numpy as jnp
from jax import lax
from jax.sharding import PartitionSpec as P

P_SIZE = 7
CXC = 2
CYC = 3
CZC = 1
NPROJ = 256
DEGREE = 4


def passed_along(value, axis, steps):
    count = lax.axis_size(axis)
    pairs = [(source, (source + steps) % count) for source in range(count)]
    return lax.ppermute(value, axis, pairs)


def spread_axis(field, axis, count):
    span = (P_SIZE - 1) * (count - 1) + 1
    slices = [
        lax.slice_in_dim(field, start, start + span, stride=P_SIZE - 1, axis=axis)
        for start in range(P_SIZE)
    ]
    return jnp.stack(slices, axis=axis + 1)


def extract(extended):
    width = extended.shape[3]
    gathered = spread_axis(extended, 2, CXC)
    gathered = spread_axis(gathered, 1, CYC)
    gathered = spread_axis(gathered, 0, CZC)
    gathered = gathered.transpose(0, 2, 4, 1, 3, 5, 6)
    return gathered.reshape(CZC * CYC * CXC, P_SIZE * P_SIZE * P_SIZE, width)


def fold_front(grouped):
    count = grouped.shape[0]
    rest = grouped.shape[2:]
    heads = grouped[:, : P_SIZE - 1]
    tails = grouped[:, P_SIZE - 1 :]
    moved = jnp.concatenate([tails, jnp.zeros((count, P_SIZE - 2) + rest, jnp.float32)], axis=1)
    empty = jnp.zeros((1, P_SIZE - 1) + rest, jnp.float32)
    total = jnp.concatenate([heads, empty], axis=0) + jnp.concatenate([empty, moved], axis=0)
    total = total.reshape(((count + 1) * (P_SIZE - 1),) + rest)
    return total[: count * (P_SIZE - 1) + 1]


def fold_axis(grouped, axis):
    moved = jnp.moveaxis(grouped, (axis, axis + 1), (0, 1))
    return jnp.moveaxis(fold_front(moved), 0, axis)


def assemble(cell_out):
    width = cell_out.shape[2]
    grouped = cell_out.reshape(CZC, CYC, CXC, P_SIZE, P_SIZE, P_SIZE, width).transpose(
        0, 3, 1, 4, 2, 5, 6
    )
    grouped = fold_axis(grouped, 4)
    grouped = fold_axis(grouped, 2)
    return fold_axis(grouped, 0)


def apply_hamiltonian(
    current,
    kinetic,
    cell_scale,
    potential,
    proj_values,
    piece_cell,
    piece_proj,
    coupling,
    center,
    halfwidth,
):
    rounded = current.astype(jnp.bfloat16)
    neighbour = passed_along(rounded[0:1], "dom", -1)
    extended = jnp.concatenate([rounded, neighbour], axis=0)
    cell_vals = extract(extended)
    cell_out = (
        jnp.einsum("pq,nqk->npk", kinetic, cell_vals, preferred_element_type=jnp.float32)
        * cell_scale[:, None, None]
    )
    picked = jnp.take(cell_vals, piece_cell, axis=0)
    piece_coef = jnp.einsum("np,npk->nk", proj_values, picked, preferred_element_type=jnp.float32)
    proj_hot = piece_proj[None, :] == jnp.arange(NPROJ, dtype=jnp.int32)[:, None]
    partial_coef = jnp.dot(
        proj_hot.astype(jnp.float32), piece_coef, precision=lax.Precision.HIGHEST
    )
    summed = lax.psum(partial_coef.astype(jnp.bfloat16), "dom").astype(jnp.float32)
    scaled = (coupling[:, None] * summed).astype(jnp.bfloat16)
    per_piece = jnp.dot(proj_hot.T.astype(jnp.bfloat16), scaled, preferred_element_type=jnp.float32)
    weighted = proj_values.astype(jnp.float32)[:, :, None] * per_piece[:, None, :]
    cell_hot = (
        piece_cell[None, :] == jnp.arange(cell_vals.shape[0], dtype=jnp.int32)[:, None]
    ).astype(jnp.float32)
    cell_out = cell_out + jnp.einsum(
        "mn,npk->mpk", cell_hot, weighted, precision=lax.Precision.HIGHEST
    )
    assembled = assemble(cell_out)
    shared = passed_along(assembled[-1:], "dom", 1)
    applied = jnp.concatenate([assembled[0:1] + shared, assembled[1:-1]], axis=0)
    return (applied + (potential[..., None] - center[0]) * current) / halfwidth[0]


def filter_block(block, operands):
    previous = block.astype(jnp.float32)
    current = apply_hamiltonian(previous, *operands)
    for step in range(DEGREE - 1):
        following = 2.0 * apply_hamiltonian(current, *operands) - previous
        previous = current
        current = following
    return current


def local(
    wave,
    kinetic,
    cell_scale,
    potential,
    proj_values,
    piece_cell,
    piece_proj,
    coupling,
    center,
    halfwidth,
):
    operands = (
        kinetic,
        cell_scale,
        potential,
        proj_values,
        piece_cell,
        piece_proj,
        coupling,
        center,
        halfwidth,
    )
    half_cols = wave.shape[3] // 2
    first = filter_block(wave[..., :half_cols], operands)
    second = filter_block(wave[..., half_cols:], operands)
    return jnp.concatenate([first, second], axis=3)


def solution(mesh):
    in_specs = (
        P("dom", None, None, "band"),
        P(),
        P("dom"),
        P("dom", None, None),
        P("dom", None),
        P("dom"),
        P("dom"),
        P(),
        P(),
        P(),
    )
    out_specs = P("dom", None, None, "band")
    return jax.shard_map(local, mesh=mesh, in_specs=in_specs, out_specs=out_specs, check_vma=False)
```

profile of v0, /device:TPU:6, one launch (start us, length us, event | category | flops | bytes accessed | tf_op | source)
XLA Modules:
  0.0 1327.0 jit_solution(2562481858828304736)
XLA Ops:
  7.5 5.6 collective-permute-start
  36.4 200.5 %all-reduce.87.cloned.1.call-done = (bf16[256,128]{1,0:T(8,128)(2,1)}, bf16[256,128]{1,0:T(8,128)(2,1)}) async-done(((bf16[256,128]{1,0:T(8,128)(2,1)}, bf16[256,128]{1,0:T(8,128)(2,1)}), (bf16[256,128]{1,0:T(8,128)(2,1)}, bf16[256,128]{1,0:T(8,128)(2,1)})) %all-reduce.87.cloned.1.call-update) | async-done | bytes 131088 | tf_op jit(solution)/shard_map/psum | solution.py:91
  258.6 5.9 collective-permute-done.1
  269.8 4.6 slice.1062
  274.4 4.6 slice.1061
  283.5 4.5 slice.1059
  288.0 4.5 slice.1058
  312.2 4.6 slice.927
  321.3 4.5 slice.925
  375.9 202.4 %all-reduce.85.cloned.1.call-done = (bf16[256,128]{1,0:T(8,128)(2,1)}, bf16[256,128]{1,0:T(8,128)(2,1)}) async-done(((bf16[256,128]{1,0:T(8,128)(2,1)}, bf16[256,128]{1,0:T(8,128)(2,1)}), (bf16[256,128]{1,0:T(8,128)(2,1)}, bf16[256,128]{1,0:T(8,128)(2,1)})) %all-reduce.85.cloned.1.call-update) | async-done | bytes 131088 | tf_op jit(solution)/shard_map/psum | solution.py:91
  608.3 5.9 collective-permute-done.3
  620.8 4.6 slice.1095
  625.4 4.6 slice.1094
  634.5 4.5 slice.1092
  639.0 4.5 slice.1091
  663.2 4.6 slice.960
  672.3 4.5 slice.958
  726.8 202.7 %all-reduce.83.cloned.1.call-done = (bf16[256,128]{1,0:T(8,128)(2,1)}, bf16[256,128]{1,0:T(8,128)(2,1)}) async-done(((bf16[256,128]{1,0:T(8,128)(2,1)}, bf16[256,128]{1,0:T(8,128)(2,1)}), (bf16[256,128]{1,0:T(8,128)(2,1)}, bf16[256,128]{1,0:T(8,128)(2,1)})) %all-reduce.83.cloned.1.call-update) | async-done | bytes 131088 | tf_op jit(solution)/shard_map/psum | solution.py:91
  959.6 5.9 collective-permute-done.5
  1009.0 4.6 slice.994
  1013.6 4.6 slice.993
  1027.2 4.6 slice.990
  1077.1 202.9 %all-reduce.81.cloned.1.call-done = (bf16[256,128]{1,0:T(8,128)(2,1)}, bf16[256,128]{1,0:T(8,128)(2,1)}) async-done(((bf16[256,128]{1,0:T(8,128)(2,1)}, bf16[256,128]{1,0:T(8,128)(2,1)}), (bf16[256,128]{1,0:T(8,128)(2,1)}, bf16[256,128]{1,0:T(8,128)(2,1)})) %all-reduce.81.cloned.1.call-update) | async-done | bytes 131088 | tf_op jit(solution)/shard_map/psum | solution.py:91
  1309.9 5.9 collective-permute-done.7
  (582 shorter events, 404.1 us)
Async XLA Ops:
  6.5 232.8 %copy-start = (bf16[343,343]{1,0:T(8,128)(2,1)S(1)}, bf16[343,343]{1,0:T(8,128)(2,1)}, u32[]{:S(2)}) copy-start(bf16[343,343]{1,0:T(8,128)(2,1)} %param.13) | copy-start | bytes 705898
  6.5 230.3 %all-reduce.87.cloned.1.call-start = ((), (), s32[]{:S(2)}) async-start(), calls=%async_computation.3 | async-start | bytes 262144 | tf_op jit(solution)/shard_map/psum | solution.py:91
  7.5 10.4 collective-permute-start
  13.2 4.8 collective-permute-start.8
  17.9 231.4 %copy-start.43 = (f32[16,343]{0,1:T(8,128)}, f32[16,343]{0,1:T(8,128)S(1)}, u32[]{:S(2)}) copy-start(f32[16,343]{0,1:T(8,128)S(1)} %copy.84) | copy-start | bytes 65860
  33.4 203.5 %copy-start.58 = (f32[256]{0:T(256)S(1)}, f32[256]{0:T(256)}, u32[]{:S(2)}) copy-start(f32[256]{0:T(256)} %param.19) | copy-start | bytes 3076
  33.4 204.6 %copy-start.59 = (s32[16]{0:T(128)S(1)}, s32[16]{0:T(128)}, u32[]{:S(2)}) copy-start(s32[16]{0:T(128)} %param.17) | copy-start | bytes 196
  35.7 542.7 %all-reduce.85.cloned.1.call-start = ((), (), s32[]{:S(2)}) async-start(), calls=%async_computation.2 | async-start | bytes 262144 | tf_op jit(solution)/shard_map/psum | solution.py:91
  257.7 6.8 collective-permute-start.1
  258.5 7.7 collective-permute-start.9
  266.9 2.0 collective-permute-start.10
  267.5 33.8 %collective-permute-start.2 = (bf16[1,19,13,128]{3,2,1,0:T(8,128)(2,1)}, bf16[1,19,13,128]{3,2,1,0:T(8,128)(2,1)}, u32[]{:S(2)}, u32[]{:S(2)}) collective-permute-start(bf16[1,19,13,128]{3,2,1,0:T(8,128)(2,1)} %slice.1188), channel_id=1, source_target_pairs={{0,31},{1,0},{2,1},{3,2},{4,3},{5,4},{6,5},{7,6},{8,7},{9,8},{10,9... | collective-permute-start | bytes 189704 | tf_op jit(solution)/shard_map/ppermute | solution.py:17
  375.5 553.9 %all-reduce.83.cloned.1.call-start = ((), (), s32[]{:S(2)}) async-start(), calls=%async_computation.1 | async-start | bytes 262144 | tf_op jit(solution)/shard_map/psum | solution.py:91
  607.4 6.8 collective-permute-start.3
  608.2 7.7 collective-permute-start.11
  617.8 2.1 collective-permute-start.12
  618.6 33.8 %collective-permute-start.4 = (bf16[1,19,13,128]{3,2,1,0:T(8,128)(2,1)}, bf16[1,19,13,128]{3,2,1,0:T(8,128)(2,1)}, u32[]{:S(2)}, u32[]{:S(2)}) collective-permute-start(bf16[1,19,13,128]{3,2,1,0:T(8,128)(2,1)} %slice.1207), channel_id=1, source_target_pairs={{0,31},{1,0},{2,1},{3,2},{4,3},{5,4},{6,5},{7,6},{8,7},{9,8},{10,9... | collective-permute-start | bytes 189704 | tf_op jit(solution)/shard_map/ppermute | solution.py:17
  726.5 553.5 %all-reduce.81.cloned.1.call-start = ((), (), s32[]{:S(2)}) async-start(), calls=%async_computation | async-start | bytes 262144 | tf_op jit(solution)/shard_map/psum | solution.py:91
  958.7 6.8 collective-permute-start.5
  959.5 7.7 collective-permute-start.13
  968.3 2.1 collective-permute-start.14
  969.0 33.7 %collective-permute-start.6 = (bf16[1,19,13,128]{3,2,1,0:T(8,128)(2,1)}, bf16[1,19,13,128]{3,2,1,0:T(8,128)(2,1)}, u32[]{:S(2)}, u32[]{:S(2)}) collective-permute-start(bf16[1,19,13,128]{3,2,1,0:T(8,128)(2,1)} %slice.1226), channel_id=1, source_target_pairs={{0,31},{1,0},{2,1},{3,2},{4,3},{5,4},{6,5},{7,6},{8,7},{9,8},{10,9... | collective-permute-start | bytes 189704 | tf_op jit(solution)/shard_map/ppermute | solution.py:17
  1309.1 6.8 collective-permute-start.7
  1309.9 7.6 collective-permute-start.15
  (56 other events, 449.8 us)
Sparse Core Ops, SparseCore 0:
  35.8 201.0 all-reduce.86
  375.6 202.7 all-reduce.84
  726.6 202.7 all-reduce.82
  1077.2 202.7 all-reduce.80
where the time goes:
time: 1350 us; the launch traced here: 1330 us
  waiting for transfers between devices  838 us (62%)
  local copies, waits for them, and re-layouts  377 us (28%)
  matrix products  48.8 us (4%)
  other arithmetic  36.6 us (3%)
  between operations  16.8 us (1%)
    psum x4, waiting for transfers between devices, apply_hamiltonian(): lax.psum(partial_coef.astype(jnp.bfloat16), 'dom').astype(jnp.float32)  809 us
    slice x56, local copies, waits for them, and re-layouts, spread_axis(): lax.slice_in_dim(field, start, start + span, stride=P_SIZE - 1, axis=axis)  191 us
    unnamed x264, local copies, waits for them, and re-layouts  69.5 us
    ppermute x16, waiting for transfers between devices, passed_along(): return lax.ppermute(value, axis, pairs)  29.7 us
  transfers between devices with their start and end apart: 20, of which 15 were waited for; matrix products, arithmetic and copies ran while one was open for 8% of the time, Pallas kernels for 0%

commit v1 on v0

--- a/solution.py
+++ b/solution.py
@@ -88,7 +88,9 @@
     partial_coef = jnp.dot(
         proj_hot.astype(jnp.float32), piece_coef, precision=lax.Precision.HIGHEST
     )
-    summed = lax.psum(partial_coef.astype(jnp.bfloat16), "dom").astype(jnp.float32)
+    summed = jnp.sum(lax.all_gather(partial_coef.astype(jnp.bfloat16), "dom"), axis=0).astype(
+        jnp.float32
+    )
     scaled = (coupling[:, None] * summed).astype(jnp.bfloat16)
     per_piece = jnp.dot(proj_hot.T.astype(jnp.bfloat16), scaled, preferred_element_type=jnp.float32)
     weighted = proj_values.astype(jnp.float32)[:, :, None] * per_piece[:, None, :]

time: 1350 us -> 838 us (0.62)
  waiting for transfers between devices: 838 us -> 472 us
  local copies, waits for them, and re-layouts: 377 us -> 234 us
    psum x4 -> x0, waiting for transfers between devices: 809 us -> none  [apply_hamiltonian(): lax.psum(partial_coef.astype(jnp.bfloat16), 'dom').astype(jnp.float32)]
    all_gather x0 -> x8, waiting for transfers between devices: none -> 422 us  [apply_hamiltonian(): lax.all_gather(partial_coef.astype(jnp.bfloat16), 'dom')]
    slice x56, local copies, waits for them, and re-layouts: 191 us -> 109 us  [spread_axis(): lax.slice_in_dim(field, start, start + span, stride=P_SIZE - 1, axis=axis)]
    unnamed x264 -> x224, local copies, waits for them, and re-layouts: 69.5 us -> 31.7 us
    ppermute x16, waiting for transfers between devices: 29.7 us -> 49.4 us  [passed_along(): return lax.ppermute(value, axis, pairs)]
    reduce_sum x0 -> x8, other arithmetic: none -> 16.3 us  [apply_hamiltonian(): jnp.sum(lax.all_gather(partial_coef.astype(jnp.bfloat16), 'dom'), axis=0)]
  transfers between devices with their start and end apart: 20 -> 24, of which waited for: 15 -> 20; matrix products, arithmetic and copies ran while one was open for 8% -> 15% of each run, Pallas kernels for 0% -> 0%
where the time goes in v1:
time: 838 us; the launch traced here: 826 us
  waiting for transfers between devices  472 us (56%)
  local copies, waits for them, and re-layouts  234 us (28%)
  other arithmetic  46.8 us (6%)
  matrix products  44.7 us (5%)
  between operations  17.4 us (2%)
  starting transfers between devices  11.4 us (1%)
    all_gather x8, waiting for transfers between devices, apply_hamiltonian(): lax.all_gather(partial_coef.astype(jnp.bfloat16), 'dom')  422 us
    slice x56, local copies, waits for them, and re-layouts, spread_axis(): lax.slice_in_dim(field, start, start + span, stride=P_SIZE - 1, axis=axis)  109 us
    ppermute x16, waiting for transfers between devices, passed_along(): return lax.ppermute(value, axis, pairs)  49.4 us
    unnamed x224, local copies, waits for them, and re-layouts  31.7 us
    reshape x16, local copies, waits for them, and re-layouts, extract(): return gathered.reshape(CZC * CYC * CXC, P_SIZE * P_SIZE * P_SIZE, width)  18.7 us
  transfers between devices with their start and end apart: 24, of which 20 were waited for; matrix products, arithmetic and copies ran while one was open for 15% of the time, Pallas kernels for 0%

profile of v1, /device:TPU:6, one launch (start us, length us, event | category | flops | bytes accessed | tf_op | source)
XLA Modules:
  0.0 825.8 jit_solution(13623882807178044205)
XLA Ops:
  7.5 5.6 collective-permute-start
  26.6 61.0 %all-gather.17.cloned.1.call-done = bf16[8192,128]{1,0:T(8,128)(2,1)} async-done(((bf16[256,128]{1,0:T(8,128)(2,1)}), bf16[8192,128]{1,0:T(8,128)(2,1)}) %all-gather.17.cloned.1.call-update) | async-done | bytes 2097168 | tf_op jit(solution)/shard_map/all_gather | solution.py:91
  125.5 4.6 slice.1025
  130.1 4.6 slice.1024
  138.6 50.5 %all-gather.19.cloned.1.call-done = bf16[8192,128]{1,0:T(8,128)(2,1)} async-done(((bf16[256,128]{1,0:T(8,128)(2,1)}), bf16[8192,128]{1,0:T(8,128)(2,1)}) %all-gather.19.cloned.1.call-update) | async-done | bytes 2097168 | tf_op jit(solution)/shard_map/all_gather | solution.py:91
  201.1 5.8 collective-permute-done.3
  213.6 4.6 slice.1028
  218.1 4.5 slice.1027
  222.7 4.6 slice.1026
  253.6 48.4 %all-gather.21.cloned.1.call-done = bf16[8192,128]{1,0:T(8,128)(2,1)} async-done(((bf16[256,128]{1,0:T(8,128)(2,1)}), bf16[8192,128]{1,0:T(8,128)(2,1)}) %all-gather.21.cloned.1.call-update) | async-done | bytes 2097168 | tf_op jit(solution)/shard_map/all_gather | solution.py:91
  317.9 5.5 collective-permute-done.5
  341.9 4.6 slice.991
  346.5 4.5 slice.990
  366.6 21.8 %all-gather.25.cloned.1.call-done = bf16[8192,128]{1,0:T(8,128)(2,1)} async-done(((bf16[256,128]{1,0:T(8,128)(2,1)}), bf16[8192,128]{1,0:T(8,128)(2,1)}) %all-gather.25.cloned.1.call-update) | async-done | bytes 2097168 | tf_op jit(solution)/shard_map/all_gather | solution.py:91
  404.8 49.5 %all-gather.23.cloned.1.call-done = bf16[8192,128]{1,0:T(8,128)(2,1)} async-done(((bf16[256,128]{1,0:T(8,128)(2,1)}), bf16[8192,128]{1,0:T(8,128)(2,1)}) %all-gather.23.cloned.1.call-update) | async-done | bytes 2097168 | tf_op jit(solution)/shard_map/all_gather | solution.py:91
  472.8 5.3 collective-permute-done.7
  493.7 63.6 %all-gather.27.cloned.1.call-done = bf16[8192,128]{1,0:T(8,128)(2,1)} async-done(((bf16[256,128]{1,0:T(8,128)(2,1)}), bf16[8192,128]{1,0:T(8,128)(2,1)}) %all-gather.27.cloned.1.call-update) | async-done | bytes 2097168 | tf_op jit(solution)/shard_map/all_gather | solution.py:91
  572.2 6.5 collective-permute-done.11
  593.7 63.6 %all-gather.29.cloned.1.call-done = bf16[8192,128]{1,0:T(8,128)(2,1)} async-done(((bf16[256,128]{1,0:T(8,128)(2,1)}), bf16[8192,128]{1,0:T(8,128)(2,1)}) %all-gather.29.cloned.1.call-update) | async-done | bytes 2097168 | tf_op jit(solution)/shard_map/all_gather | solution.py:91
  672.4 6.5 collective-permute-done.13
  696.1 4.5 slice.1125
  700.6 4.5 slice.1124
  728.7 63.6 %all-gather.31.cloned.1.call-done = bf16[8192,128]{1,0:T(8,128)(2,1)} async-done(((bf16[256,128]{1,0:T(8,128)(2,1)}), bf16[8192,128]{1,0:T(8,128)(2,1)}) %all-gather.31.cloned.1.call-update) | async-done | bytes 2097168 | tf_op jit(solution)/shard_map/all_gather | solution.py:91
  809.6 6.5 collective-permute-done.15
  (565 shorter events, 303.6 us)
Async XLA Ops:
  6.5 81.1 %all-gather.17.cloned.1.call-start = ((), (), s32[]{:S(2)}) async-start(), calls=%async_computation | async-start | bytes 2162688 | tf_op jit(solution)/shard_map/all_gather | solution.py:91
  7.5 9.0 %collective-permute-start = (bf16[1,19,13,128]{3,2,1,0:T(8,128)(2,1)S(1)}, bf16[1,19,13,128]{3,2,1,0:T(8,128)(2,1)S(1)}, u32[]{:S(2)}, u32[]{:S(2)}) collective-permute-start(bf16[1,19,13,128]{3,2,1,0:T(8,128)(2,1)S(1)} %get-tuple-element.14), channel_id=1, source_target_pairs={{0,31},{1,0},{2,1},{3,2},{4,3},{5,4},{6,5},{7,6},{8,7},{9,8},{10,9... | collective-permute-start | bytes 189704 | tf_op jit(solution)/shard_map/ppermute | solution.py:17
  13.2 3.4 collective-permute-start.8
  24.7 164.4 %all-gather.19.cloned.1.call-start = ((), (), s32[]{:S(2)}) async-start(), calls=%async_computation.1 | async-start | bytes 2162688 | tf_op jit(solution)/shard_map/all_gather | solution.py:91
  96.5 6.8 collective-permute-start.1
  104.6 2.3 collective-permute-start.2
  125.5 176.6 %all-gather.21.cloned.1.call-start = ((), (), s32[]{:S(2)}) async-start(), calls=%async_computation.2 | async-start | bytes 2162688 | tf_op jit(solution)/shard_map/all_gather | solution.py:91
  200.1 6.8 collective-permute-start.3
  208.4 18.9 %collective-permute-start.4 = (bf16[1,19,13,128]{3,2,1,0:T(8,128)(2,1)S(1)}, bf16[1,19,13,128]{3,2,1,0:T(8,128)(2,1)S(1)}, u32[]{:S(2)}, u32[]{:S(2)}) collective-permute-start(bf16[1,19,13,128]{3,2,1,0:T(8,128)(2,1)S(1)} %slice.1207), channel_id=1, source_target_pairs={{0,31},{1,0},{2,1},{3,2},{4,3},{5,4},{6,5},{7,6},{8,7},{9,8},{10,9... | collective-permute-start | bytes 189704 | tf_op jit(solution)/shard_map/ppermute | solution.py:17
  238.6 149.8 %all-gather.25.cloned.1.call-start = ((), (), s32[]{:S(2)}) async-start(), calls=%async_computation.4 | async-start | bytes 2162688 | tf_op jit(solution)/shard_map/all_gather | solution.py:91
  316.6 6.8 collective-permute-start.5
  324.1 2.0 collective-permute-start.6
  325.0 129.3 %all-gather.23.cloned.1.call-start = ((), (), s32[]{:S(2)}) async-start(), calls=%async_computation.3 | async-start | bytes 2162688 | tf_op jit(solution)/shard_map/all_gather | solution.py:91
  366.6 190.7 %all-gather.27.cloned.1.call-start = ((), (), s32[]{:S(2)}) async-start(), calls=%async_computation.5 | async-start | bytes 2162688 | tf_op jit(solution)/shard_map/all_gather | solution.py:91
  404.3 67.3 %collective-permute-start.9 = (f32[1,19,13,128]{3,2,1,0:T(8,128)}, f32[1,19,13,128]{3,2,1,0:T(8,128)}, u32[]{:S(2)}, u32[]{:S(2)}) collective-permute-start(f32[1,19,13,128]{3,2,1,0:T(8,128)} %slice.1261), channel_id=1, source_target_pairs={{0,1},{1,2},{2,3},{3,4},{4,5},{5,6},{6,7},{7,8},{8,9},{9,10},{10,1... | collective-permute-start | bytes 379400 | tf_op jit(solution)/shard_map/ppermute | solution.py:17
  471.3 6.8 collective-permute-start.7
  479.9 2.4 collective-permute-start.10
  493.6 163.7 %all-gather.29.cloned.1.call-start = ((), (), s32[]{:S(2)}) async-start(), calls=%async_computation.6 | async-start | bytes 2162688 | tf_op jit(solution)/shard_map/all_gather | solution.py:91
  571.8 6.8 collective-permute-start.11
  580.1 2.2 collective-permute-start.12
  593.6 198.7 %all-gather.31.cloned.1.call-start = ((), (), s32[]{:S(2)}) async-start(), calls=%async_computation.7 | async-start | bytes 2162688 | tf_op jit(solution)/shard_map/all_gather | solution.py:91
  671.9 7.1 collective-permute-start.13
  679.4 2.1 collective-permute-start.14
  809.3 6.8 collective-permute-start.15
  (40 other events, 806.6 us)
Sparse Core Ops, SparseCore 0:
  24.8 62.7 all-gather.16
  125.6 63.4 all-gather.18
  238.8 63.2 all-gather.20
  325.1 63.2 all-gather.24
  390.1 64.0 all-gather.22
  493.7 63.5 all-gather.26
  593.7 63.5 all-gather.28
  728.8 63.4 all-gather.30
